TPU v7x, 32 devices: a whole 2x2x4 slice. The times are simulated.
32 devices in a mesh: tm: 16 (over z, y, x), rows: 2 (over core).
Axes of the slice: x: 2, y: 2, z: 4, core: 2. Of those that a mesh axis runs over, the one named last changes fastest.
Arguments:
- observed: float32 [192, 512, 128], P('tm', 'rows'), may hold values from -12 to 12
- gain: float32 [192, 512], P('tm'), may hold values from 2.5e-05 to 0.525
- smooth_gain: float32 [192, 512], P('tm'), may hold values from 0.475 to 0.999975
- dynamics: float32 [512, 512], replicated, may hold values from -0.0021213203 to 0.9998
- pattern: int32 [8, 8], replicated, may hold values from 0 to 1, as said below
- initial: float32 [512, 128], P('rows'), may hold values from -6 to 6
- lengths: int32 [16], P('tm'), may hold values from 1 to 12, 144 in all
Outputs:
- filtered: float32 [192, 512, 128], P('tm', 'rows')
- smoothed: float32 [192, 512, 128], P('tm', 'rows')
Inputs may be any that keep to these rules, and one draw needn't show every extreme that they name: `pattern`: 0 or 1; every diagonal entry is 1. The first lengths[d] of the 12 slots of time device d are live.
All inputs are finite; a program needn't handle non-finite values.
Results may differ from a plain program's by a relative error of at most 0.0003.
Values sent between devices are 32-bit elements; how exact they have to be, the bound alone decides.
No kernel may reach another device: no remote copies, remote signals or barrier semaphores. Data moves between devices by JAX's collectives and lax.ppermute only.
A program may use at most 64 MiB of HBM per device.

v0:
```python
import jax
import jax.numpy as jnp
from jax import lax
from jax.experimental.layout import Layout, with_layout_constraint
from jax.sharding import PartitionSpec as P

HIGHEST = lax.Precision.HIGHEST


def passed_along(block, axis, distance):
    devices = range(lax.axis_size(axis))
    route = [(i - distance, i) for i in devices if i - distance in devices]
    return lax.ppermute(block, axis, route)


def rows_whole(part, axis):
    count = lax.axis_size("rows")
    if count != 2:
        return lax.all_gather(part, "rows", axis=axis, tiled=True)
    other = lax.ppermute(part, "rows", [(0, 1), (1, 0)])
    first_half = lax.axis_index("rows") == 0
    lower = jnp.where(first_half, part, other)
    upper = jnp.where(first_half, other, part)
    return jnp.concatenate([lower, upper], axis=axis)


def matmul(left, right):
    return jnp.dot(left, right, precision=HIGHEST, preferred_element_type=jnp.float32)


def left_transposed(left, right):
    return lax.dot_general(
        left, right, (((0,), (0,)), ((), ())), precision=HIGHEST, preferred_element_type=jnp.float32
    )


def right_transposed(left, right):
    return lax.dot_general(
        left, right, (((1,), (1,)), ((), ())), precision=HIGHEST, preferred_element_type=jnp.float32
    )


def batched(left, right):
    return lax.dot_general(
        left, right, (((2,), (1,)), ((0,), (0,))), precision=HIGHEST, preferred_element_type=jnp.float32
    )


def masked_dynamics(pattern, dynamics):
    blocks = pattern.shape[0]
    block_width = dynamics.shape[0] // blocks
    spread = jnp.broadcast_to(
        pattern.astype(dynamics.dtype)[:, None, :, None], (blocks, block_width, blocks, block_width)
    )
    return dynamics * spread.reshape(dynamics.shape)


def lead_chain(start_rows, scales, live_slots, apply, backwards):
    def advance(lead, step_inputs):
        scale, is_live = step_inputs
        fresh = apply(lead * scale[None, :])
        return jnp.where(is_live, fresh, lead), lead

    return lax.scan(advance, start_rows, (scales, live_slots), reverse=backwards, unroll=True)


def lead_levels(lead, direction, devices, time_index):
    levels = (devices - 1).bit_length()
    leads = [lead]
    for tree_level in range(levels - 1):
        distance = 1 << tree_level
        far = rows_whole(passed_along(leads[-1], "tm", direction * distance), 0)
        has_peer = time_index >= distance if direction > 0 else time_index < devices - distance
        leads.append(jnp.where(has_peer, matmul(leads[-1], far), leads[-1]))
    return leads[:levels]


def offset_levels(offset, leads, direction, devices, time_index):
    for tree_level, lead in enumerate(leads):
        distance = 1 << tree_level
        far = rows_whole(passed_along(offset, "tm", direction * distance), 0)
        has_peer = time_index >= distance if direction > 0 else time_index < devices - distance
        offset = jnp.where(has_peer, offset + matmul(lead, far), offset)
    return offset


def per_device(observed, gain, smooth_gain, dynamics, pattern, initial, lengths):
    steps_local, row_count, tracks = observed.shape
    devices = lax.axis_size("tm")
    time_index = lax.axis_index("tm")
    row_start = lax.axis_index("rows") * row_count
    transition = masked_dynamics(pattern, dynamics)
    transposed = with_layout_constraint(transition.T, Layout(major_to_minor=(0, 1)))
    state_width = transition.shape[0]
    live_slots = jnp.arange(steps_local, dtype=jnp.int32) < lengths[0]
    column_ids = jnp.arange(state_width, dtype=jnp.int32)
    row_ids = row_start + jnp.arange(row_count, dtype=jnp.int32)
    identity_rows = (column_ids[None, :] == row_ids[:, None]).astype(jnp.float32)
    start_whole = lax.all_gather(initial, "rows", axis=0, tiled=True)
    obs_whole = lax.all_gather(observed, "rows", axis=1, tiled=True)
    at_first = time_index == 0
    at_last = time_index == devices - 1

    fwd_lead, fwd_before = lead_chain(
        identity_rows, 1.0 - gain, live_slots, lambda x: matmul(x, transition), True
    )
    fwd_leads = lead_levels(jnp.where(at_first, 0.0, fwd_lead), 1, devices, time_index)
    inputs = jnp.where(live_slots[:, None, None], gain[:, :, None] * obs_whole, 0.0)
    fwd_offset = jnp.sum(batched(fwd_before, inputs), axis=0)
    fwd_offset = jnp.where(at_first, fwd_offset + matmul(fwd_lead, start_whole), fwd_offset)
    fwd_inclusive = offset_levels(fwd_offset, fwd_leads, 1, devices, time_index)
    entry_rows = jnp.where(at_first, initial, passed_along(fwd_inclusive, "tm", 1))
    entry_whole = rows_whole(entry_rows, 0)

    back_lead, back_before = lead_chain(
        identity_rows, smooth_gain, live_slots, lambda x: matmul(x, transposed), False
    )
    back_leads = lead_levels(jnp.where(at_last, 0.0, back_lead), -1, devices, time_index)

    def forward(mean_whole, step_inputs):
        obs_now, rate_now, is_live = step_inputs
        image_now = matmul(transition, mean_whole)
        fresh = (1.0 - rate_now)[:, None] * image_now + rate_now[:, None] * obs_now
        mean_next = jnp.where(is_live, fresh, mean_whole)
        return mean_next, (mean_next, image_now)

    final_mean, (filtered_whole, images) = lax.scan(
        forward, entry_whole, (obs_whole, gain, live_slots), unroll=True
    )
    terminal = matmul(transition, final_mean)
    image_all = jnp.concatenate([images[1:], terminal[None]], axis=0)
    pulled = jnp.einsum("ij,tjk->tik", transposed, image_all, precision=HIGHEST,
                        preferred_element_type=jnp.float32)
    offsets = filtered_whole - smooth_gain[:, :, None] * pulled

    live_offsets = jnp.where(live_slots[:, None, None], offsets, 0.0)
    back_offset = jnp.sum(batched(back_before, live_offsets), axis=0)
    back_offset = jnp.where(at_last, back_offset + matmul(back_lead, terminal), back_offset)
    back_inclusive = offset_levels(back_offset, back_leads, -1, devices, time_index)
    terminal_rows = lax.dynamic_slice_in_dim(terminal, row_start, row_count, 0)
    after_rows = jnp.where(at_last, terminal_rows, passed_along(back_inclusive, "tm", -1))
    after_whole = rows_whole(after_rows, 0)

    def backward(later_whole, step_inputs):
        offset_now, keep_now, is_live = step_inputs
        fresh = keep_now[:, None] * matmul(transposed, later_whole) + offset_now
        smooth_now = jnp.where(is_live, fresh, later_whole)
        return smooth_now, smooth_now

    first_whole, smoothed_whole = lax.scan(
        backward, after_whole, (offsets, smooth_gain, live_slots), reverse=True, unroll=True
    )
    filtered = lax.dynamic_slice_in_dim(filtered_whole, row_start, row_count, 1)
    smoothed = lax.dynamic_slice_in_dim(smoothed_whole, row_start, row_count, 1)
    return (filtered, smoothed)


def solution(mesh):
    placed = (
        P("tm", "rows", None),
        P("tm", None),
        P("tm", None),
        P(),
        P(),
        P("rows", None),
        P("tm"),
    )
    return jax.shard_map(
        per_device,
        mesh=mesh,
        in_specs=placed,
        out_specs=(P("tm", "rows", None), P("tm", "rows", None)),
        check_vma=False,
    )
```

profile of v0, /device:TPU:7, one launch (start us, length us, event | category | flops | bytes accessed | tf_op | source)
XLA Modules:
  0.0 329.8 jit_solution(2598821250726902152)
XLA Ops:
  7.9 2.5 copy.10
  13.6 1.7 mul.554
  15.4 1.8 convolution_select_fusion.29
  20.4 1.7 convolution_select_fusion.26
  22.1 1.8 convolution_select_fusion.25
  23.9 1.7 convolution_select_fusion.24
  27.2 1.7 convolution_select_fusion.22
  28.9 1.7 convolution_select_fusion.21
  30.7 1.8 convolution_select_fusion.20
  32.4 2.7 bitcast_dynamic-update-slice_fusion.21
  35.2 2.5 broadcast_select_fusion.1
  37.7 3.1 collective-permute-start.2
  50.5 2.5 bitcast_dynamic-update-slice_fusion.10
  53.0 2.4 bitcast_dynamic-update-slice_fusion.9
  55.4 2.5 bitcast_dynamic-update-slice_fusion.8
  58.0 2.5 bitcast_dynamic-update-slice_fusion.7
  60.5 2.5 bitcast_dynamic-update-slice_fusion.6
  63.0 2.5 bitcast_dynamic-update-slice_fusion.5
  65.5 2.5 bitcast_dynamic-update-slice_fusion.4
  68.0 2.6 bitcast_dynamic-update-slice_fusion.3
  70.5 2.5 bitcast_dynamic-update-slice_fusion.2
  73.0 2.4 bitcast_dynamic-update-slice_fusion.1
  75.4 2.5 bitcast_dynamic-update-slice_fusion
  78.0 12.3 %broadcast_select_fusion = (f32[256,512]{1,0:T(8,128)S(1)}, f32[256,512]{1,0:T(8,128)S(1)}) fusion(pred[]{:T(512)S(6)} %eq.58, f32[256,512]{1,0:T(8,128)S(1)} %get-tuple-element.146, f32[512,512]{0,1:T(8,128)S(1)} %mul.554, f32[512]{0:T(512)S(1)} %bitcast.525, pred[]{:T(512)} %bitcast.13), kind=kOutput, calls=%fused_computation.343 | convolution fusion | flops 805699584 | bytes 2623490 | tf_op jit(solution)/shard_map/eval_jaxpr/dot_general | solution.py:28
  90.3 2.2 collective-permute-start.18
  97.9 2.0 all_gather.7
  104.6 3.2 collective-permute-start.6
  107.9 9.1 %fusion.48 = f32[256,128]{1,0:T(8,128)S(1)} fusion(f32[12,256,512]{2,1,0:T(8,128)} %get-tuple-element.104, f32[12,512,128]{2,1,0:T(8,128)} %all-gather.2.cloned.1.call-done, f32[12,512]{1,0:T(8,128)} %param.8, pred[12]{0:T(512)(128)(4,1)S(1)} %iota_compare_fusion.4), kind=kOutput, calls=%fused_computation.102 | convolution fusion | flops 2417491968 | bytes 9592844 | tf_op jit(solution)/shard_map/dot_general | solution.py:44
  117.5 4.0 %collective-permute-start = (f32[256,128]{1,0:T(8,128)S(1)}, f32[256,128]{1,0:T(8,128)S(1)}, u32[]{:S(2)}, u32[]{:S(2)}) collective-permute-start(f32[256,128]{1,0:T(8,128)S(1)} %fusion.47), channel_id=1, source_target_pairs={{0,2},{2,4},{4,6},{6,8},{8,10},{10,12},{12,14},{14,16},{16,18},{18... | collective-permute-start | bytes 393224 | tf_op jit(solution)/shard_map/ppermute | solution.py:13
  122.9 2.1 collective-permute-done
  129.6 3.4 %collective-permute-start.4 = (f32[256,128]{1,0:T(8,128)S(1)}, f32[256,128]{1,0:T(8,128)S(1)}, u32[]{:S(2)}, u32[]{:S(2)}) collective-permute-start(f32[256,128]{1,0:T(8,128)S(1)} %fusion.46), channel_id=1, source_target_pairs={{0,4},{2,6},{4,8},{6,10},{8,12},{10,14},{12,16},{14,18},{16,20},{1... | collective-permute-start | bytes 393224 | tf_op jit(solution)/shard_map/ppermute | solution.py:13
  134.3 1.9 collective-permute-done.4
  138.4 4.1 %collective-permute-start.10 = (f32[256,512]{1,0:T(8,128)S(1)}, f32[256,512]{1,0:T(8,128)}, u32[]{:S(2)}, u32[]{:S(2)}) collective-permute-start(f32[256,512]{1,0:T(8,128)S(1)} %convolution_select_fusion.4), channel_id=1, source_target_pairs={{0,8},{2,10},{4,12},{6,14},{8,16},{10,18},{12,20},{14,22},{16,24},... | collective-permute-start | bytes 1572872 | tf_op jit(solution)/shard_map/ppermute | solution.py:13
  143.1 2.3 collective-permute-start.8
  146.1 6.8 %collective-permute-done.10 = f32[256,512]{1,0:T(8,128)} collective-permute-done((f32[256,512]{1,0:T(8,128)S(1)}, f32[256,512]{1,0:T(8,128)}, u32[]{:S(2)}, u32[]{:S(2)}) %collective-permute-start.10) | collective-permute-done | bytes 524320 | tf_op jit(solution)/shard_map/ppermute | solution.py:13
  160.2 5.1 %collective-permute-start.12 = (f32[256,128]{1,0:T(8,128)S(1)}, f32[256,128]{1,0:T(8,128)S(1)}, u32[]{:S(2)}, u32[]{:S(2)}) collective-permute-start(f32[256,128]{1,0:T(8,128)S(1)} %fusion.44), channel_id=1, source_target_pairs={{0,16},{2,18},{4,20},{6,22},{8,24},{10,26},{12,28},{14,30},{1,17},... | collective-permute-start | bytes 393224 | tf_op jit(solution)/shard_map/ppermute | solution.py:13
  170.7 8.9 %collective-permute-start.14 = (f32[256,128]{1,0:T(8,128)S(1)}, f32[256,128]{1,0:T(8,128)S(1)}, u32[]{:S(2)}, u32[]{:S(2)}) collective-permute-start(f32[256,128]{1,0:T(8,128)S(1)} %fusion.43), channel_id=1, source_target_pairs={{0,2},{2,4},{4,6},{6,8},{8,10},{10,12},{12,14},{14,16},{16,18},{18... | collective-permute-start | bytes 393224 | tf_op jit(solution)/shard_map/ppermute | solution.py:13
  184.5 2.3 collective-permute-start.22
  186.9 2.5 bitcast_dynamic-update-slice_fusion.56
  189.4 2.4 bitcast_dynamic-update-slice_fusion.55
  191.9 2.5 bitcast_dynamic-update-slice_fusion.54
  194.5 2.5 bitcast_dynamic-update-slice_fusion.53
  197.0 2.5 bitcast_dynamic-update-slice_fusion.52
  199.5 2.4 bitcast_dynamic-update-slice_fusion.51
  202.0 2.6 bitcast_dynamic-update-slice_fusion.50
  204.7 2.5 bitcast_dynamic-update-slice_fusion.49
  207.2 2.5 bitcast_dynamic-update-slice_fusion.48
  209.7 2.4 bitcast_dynamic-update-slice_fusion.47
  212.1 2.4 bitcast_dynamic-update-slice_fusion.46
  214.6 2.5 bitcast_dynamic-update-slice_fusion.45
  217.2 1.8 bitcast_dynamic-update-slice_fusion.33
  219.0 6.4 %bitcast_subtract_fusion = f32[12,512,128]{2,1,0:T(8,128)S(1)} fusion(f32[12,512,128]{2,1,0:T(8,128)S(1)} %get-tuple-element.2, f32[12,512,128]{2,1,0:T(8,128)S(1)} %get-tuple-element.123, f32[12,512]{1,0:T(8,128)S(1)} %copy-done.13, f32[512,512]{0,1:T(8,128)S(1)} %mul.554), kind=kOutput, calls=%fused_computation | convolution fusion | flops 4833411072 | bytes 10510336 | tf_op jit(solution)/shard_map/ij,tjk->tik/dot_general | solution.py:132
  225.4 5.1 %fusion.51 = f32[256,128]{1,0:T(8,128)S(1)} fusion(f32[12,256,512]{2,1,0:T(8,128)S(1)} %bitcast.478, f32[12,512,128]{2,1,0:T(8,128)S(1)} %bitcast_subtract_fusion, pred[12]{0:T(512)(128)(4,1)S(1)} %iota_compare_fusion.4), kind=kOutput, calls=%fused_computation.103 | convolution fusion | flops 2416705536 | bytes 9568268 | tf_op jit(solution)/shard_map/dot_general | solution.py:44
  231.2 1.9 collective-permute-start.16
  233.1 7.8 %collective-permute-done.16 = f32[256,128]{1,0:T(8,128)S(1)} collective-permute-done((f32[256,128]{1,0:T(8,128)S(1)}, f32[256,128]{1,0:T(8,128)S(1)}, u32[]{:S(2)}, u32[]{:S(2)}) %collective-permute-start.16) | collective-permute-done | bytes 131104 | tf_op jit(solution)/shard_map/ppermute | solution.py:13
  243.1 1.9 collective-permute-start.20
  246.2 4.4 %collective-permute-done.20 = f32[256,128]{1,0:T(8,128)S(1)} collective-permute-done((f32[256,128]{1,0:T(8,128)S(1)}, f32[256,128]{1,0:T(8,128)S(1)}, u32[]{:S(2)}, u32[]{:S(2)}) %collective-permute-start.20) | collective-permute-done | bytes 131104 | tf_op jit(solution)/shard_map/ppermute | solution.py:13
  256.1 15.0 %collective-permute-done.24 = f32[256,128]{1,0:T(8,128)S(1)} collective-permute-done((f32[256,128]{1,0:T(8,128)S(1)}, f32[256,128]{1,0:T(8,128)S(1)}, u32[]{:S(2)}, u32[]{:S(2)}) %collective-permute-start.24) | collective-permute-done | bytes 131104 | tf_op jit(solution)/shard_map/ppermute | solution.py:13
  275.0 9.1 %collective-permute-done.28 = f32[256,128]{1,0:T(8,128)S(1)} collective-permute-done((f32[256,128]{1,0:T(8,128)S(1)}, f32[256,128]{1,0:T(8,128)S(1)}, u32[]{:S(2)}, u32[]{:S(2)}) %collective-permute-start.28) | collective-permute-done | bytes 131104 | tf_op jit(solution)/shard_map/ppermute | solution.py:13
  286.9 2.5 collective-permute-start.30
  289.4 5.9 %collective-permute-done.30 = f32[256,128]{1,0:T(8,128)S(1)} collective-permute-done((f32[256,128]{1,0:T(8,128)S(1)}, f32[256,128]{1,0:T(8,128)S(1)}, u32[]{:S(2)}, u32[]{:S(2)}) %collective-permute-start.30) | collective-permute-done | bytes 131104 | tf_op jit(solution)/shard_map/ppermute | solution.py:13
  297.6 2.6 fusion.35
  300.2 2.5 fusion.33
  320.9 1.9 constant_dynamic-slice_fusion
  (277 shorter events, 92.7 us)
Async XLA Ops:
  7.2 100.6 %all-gather.2.cloned.1.call-start = ((), (), s32[]{:S(2)}) async-start(), calls=%async_computation | async-start | bytes 4718592 | tf_op jit(solution)/shard_map/all_gather | solution.py:100
  37.7 58.4 %collective-permute-start.2 = (f32[256,512]{1,0:T(8,128)S(1)}, f32[256,512]{1,0:T(8,128)S(1)}, u32[]{:S(2)}, u32[]{:S(2)}) collective-permute-start(f32[256,512]{1,0:T(8,128)S(1)} %get-tuple-element.119), channel_id=1, source_target_pairs={{0,2},{2,4},{4,6},{6,8},{8,10},{10,12},{12,14},{14,16},{16,18},{18... | collective-permute-start | bytes 1572872 | tf_op jit(solution)/shard_map/ppermute | solution.py:13
  50.4 10.1 %copy-start.16 = (f32[1,512]{1,0:T(1,128)}, f32[1,512]{1,0:T(1,128)S(1)}, u32[]{:S(2)}) copy-start(f32[1,512]{1,0:T(1,128)S(1)} %get-tuple-element.74) | copy-start | bytes 6148
  50.4 12.6 %copy-start.18 = (f32[1,512]{1,0:T(1,128)}, f32[1,512]{1,0:T(1,128)S(1)}, u32[]{:S(2)}) copy-start(f32[1,512]{1,0:T(1,128)S(1)} %get-tuple-element.73) | copy-start | bytes 6148
  50.4 15.0 %copy-start.20 = (f32[1,512]{1,0:T(1,128)}, f32[1,512]{1,0:T(1,128)S(1)}, u32[]{:S(2)}) copy-start(f32[1,512]{1,0:T(1,128)S(1)} %get-tuple-element.72) | copy-start | bytes 6148
  50.4 17.5 %copy-start.22 = (f32[1,512]{1,0:T(1,128)}, f32[1,512]{1,0:T(1,128)S(1)}, u32[]{:S(2)}) copy-start(f32[1,512]{1,0:T(1,128)S(1)} %get-tuple-element.71) | copy-start | bytes 6148
  50.4 20.1 %copy-start.24 = (f32[1,512]{1,0:T(1,128)}, f32[1,512]{1,0:T(1,128)S(1)}, u32[]{:S(2)}) copy-start(f32[1,512]{1,0:T(1,128)S(1)} %get-tuple-element.70) | copy-start | bytes 6148
  50.4 22.6 %copy-start.26 = (f32[1,512]{1,0:T(1,128)}, f32[1,512]{1,0:T(1,128)S(1)}, u32[]{:S(2)}) copy-start(f32[1,512]{1,0:T(1,128)S(1)} %get-tuple-element.69) | copy-start | bytes 6148
  50.4 25.0 %copy-start.28 = (f32[1,512]{1,0:T(1,128)}, f32[1,512]{1,0:T(1,128)S(1)}, u32[]{:S(2)}) copy-start(f32[1,512]{1,0:T(1,128)S(1)} %get-tuple-element.68) | copy-start | bytes 6148
  50.5 27.5 %copy-start.52 = (f32[1,512]{1,0:T(1,128)}, f32[1,512]{1,0:T(1,128)S(1)}, u32[]{:S(2)}) copy-start(f32[1,512]{1,0:T(1,128)S(1)} %get-tuple-element.67) | copy-start | bytes 6148
  75.4 22.5 %copy-start.6 = (f32[256,128]{1,0:T(8,128)S(1)}, f32[256,128]{1,0:T(8,128)}, u32[]{:S(2)}) copy-start(f32[256,128]{1,0:T(8,128)} %param.12) | copy-start | bytes 393220
  90.3 66.8 %collective-permute-start.18 = (f32[256,512]{1,0:T(8,128)S(1)}, f32[256,512]{1,0:T(8,128)}, u32[]{:S(2)}, u32[]{:S(2)}) collective-permute-start(f32[256,512]{1,0:T(8,128)S(1)} %get-tuple-element.147), channel_id=1, source_target_pairs={{2,0},{4,2},{6,4},{8,6},{10,8},{12,10},{14,12},{16,14},{18,16},{20... | collective-permute-start | bytes 1572872 | tf_op jit(solution)/shard_map/ppermute | solution.py:13
  96.1 6.4 %collective-permute-start.3 = (f32[256,512]{1,0:T(8,128)S(1)}, f32[256,512]{1,0:T(8,128)}, u32[]{:S(2)}, u32[]{:S(2)}) collective-permute-start(f32[256,512]{1,0:T(8,128)S(1)} %collective-permute-done.2), channel_id=1, source_target_pairs={{0,1},{1,0},{2,3},{3,2},{4,5},{5,4},{6,7},{7,6},{8,9},{9,8},{10,11... | collective-permute-start | bytes 1572872 | tf_op jit(solution)/shard_map/ppermute | solution.py:20
  104.6 17.5 %collective-permute-start.6 = (f32[256,512]{1,0:T(8,128)S(1)}, f32[256,512]{1,0:T(8,128)}, u32[]{:S(2)}, u32[]{:S(2)}) collective-permute-start(f32[256,512]{1,0:T(8,128)S(1)} %convolution_select_fusion.5), channel_id=1, source_target_pairs={{0,4},{2,6},{4,8},{6,10},{8,12},{10,14},{12,16},{14,18},{16,20},{1... | collective-permute-start | bytes 1572872 | tf_op jit(solution)/shard_map/ppermute | solution.py:13
  107.8 9.1 %copy-start.5 = (f32[256,512]{1,0:T(8,128)S(1)}, f32[256,512]{1,0:T(8,128)}, u32[]{:S(2)}) copy-start(f32[256,512]{1,0:T(8,128)} %get-tuple-element.120) | copy-start | bytes 1572868
  107.8 13.7 %copy-start.36 = (f32[1,512]{1,0:T(1,128)S(1)}, f32[1,512]{1,0:T(1,128)}, u32[]{:S(2)}) copy-start(f32[1,512]{1,0:T(1,128)} %get-tuple-element.81) | copy-start | bytes 6148
  107.8 18.1 %copy-start.34 = (f32[1,512]{1,0:T(1,128)S(1)}, f32[1,512]{1,0:T(1,128)}, u32[]{:S(2)}) copy-start(f32[1,512]{1,0:T(1,128)} %get-tuple-element.80) | copy-start | bytes 6148
  117.5 7.4 %collective-permute-start = (f32[256,128]{1,0:T(8,128)S(1)}, f32[256,128]{1,0:T(8,128)S(1)}, u32[]{:S(2)}, u32[]{:S(2)}) collective-permute-start(f32[256,128]{1,0:T(8,128)S(1)} %fusion.47), channel_id=1, source_target_pairs={{0,2},{2,4},{4,6},{6,8},{8,10},{10,12},{12,14},{14,16},{16,18},{18... | collective-permute-start | bytes 393224 | tf_op jit(solution)/shard_map/ppermute | solution.py:13
  122.1 10.8 %collective-permute-start.7 = (f32[256,512]{1,0:T(8,128)}, f32[256,512]{1,0:T(8,128)}, u32[]{:S(2)}, u32[]{:S(2)}) collective-permute-start(f32[256,512]{1,0:T(8,128)} %collective-permute-done.6), channel_id=1, source_target_pairs={{0,1},{1,0},{2,3},{3,2},{4,5},{5,4},{6,7},{7,6},{8,9},{9,8},{10,11... | collective-permute-start | bytes 1572872 | tf_op jit(solution)/shard_map/ppermute | solution.py:20
  124.9 2.1 collective-permute-start.1
  129.5 15.9 %copy-start.32 = (f32[1,512]{1,0:T(1,128)S(1)}, f32[1,512]{1,0:T(1,128)}, u32[]{:S(2)}) copy-start(f32[1,512]{1,0:T(1,128)} %get-tuple-element.90) | copy-start | bytes 6148
  129.5 27.0 %copy-start.30 = (f32[1,512]{1,0:T(1,128)S(1)}, f32[1,512]{1,0:T(1,128)}, u32[]{:S(2)}) copy-start(f32[1,512]{1,0:T(1,128)} %get-tuple-element.79) | copy-start | bytes 6148
  129.6 6.6 %collective-permute-start.4 = (f32[256,128]{1,0:T(8,128)S(1)}, f32[256,128]{1,0:T(8,128)S(1)}, u32[]{:S(2)}, u32[]{:S(2)}) collective-permute-start(f32[256,128]{1,0:T(8,128)S(1)} %fusion.46), channel_id=1, source_target_pairs={{0,4},{2,6},{4,8},{6,10},{8,12},{10,14},{12,16},{14,18},{16,20},{1... | collective-permute-start | bytes 393224 | tf_op jit(solution)/shard_map/ppermute | solution.py:13
  136.1 6.4 %collective-permute-start.5 = (f32[256,128]{1,0:T(8,128)S(1)}, f32[256,128]{1,0:T(8,128)S(1)}, u32[]{:S(2)}, u32[]{:S(2)}) collective-permute-start(f32[256,128]{1,0:T(8,128)S(1)} %collective-permute-done.4), channel_id=1, source_target_pairs={{0,1},{1,0},{2,3},{3,2},{4,5},{5,4},{6,7},{7,6},{8,9},{9,8},{10,11... | collective-permute-start | bytes 393224 | tf_op jit(solution)/shard_map/ppermute | solution.py:20
  138.4 14.5 %collective-permute-start.10 = (f32[256,512]{1,0:T(8,128)S(1)}, f32[256,512]{1,0:T(8,128)}, u32[]{:S(2)}, u32[]{:S(2)}) collective-permute-start(f32[256,512]{1,0:T(8,128)S(1)} %convolution_select_fusion.4), channel_id=1, source_target_pairs={{0,8},{2,10},{4,12},{6,14},{8,16},{10,18},{12,20},{14,22},{16,24},... | collective-permute-start | bytes 1572872 | tf_op jit(solution)/shard_map/ppermute | solution.py:13
  143.1 9.8 %copy-start.7 = (f32[256,128]{1,0:T(8,128)}, f32[256,128]{1,0:T(8,128)S(1)}, u32[]{:S(2)}) copy-start(f32[256,128]{1,0:T(8,128)S(1)} %fusion.45) | copy-start | bytes 393220
  143.1 12.6 %collective-permute-start.8 = (f32[256,128]{1,0:T(8,128)S(1)}, f32[256,128]{1,0:T(8,128)S(1)}, u32[]{:S(2)}, u32[]{:S(2)}) collective-permute-start(f32[256,128]{1,0:T(8,128)S(1)} %fusion.45), channel_id=1, source_target_pairs={{0,8},{2,10},{4,12},{6,14},{8,16},{10,18},{12,20},{14,22},{16,24},... | collective-permute-start | bytes 393224 | tf_op jit(solution)/shard_map/ppermute | solution.py:13
  152.9 12.4 %collective-permute-start.11 = (f32[256,512]{1,0:T(8,128)}, f32[256,512]{1,0:T(8,128)}, u32[]{:S(2)}, u32[]{:S(2)}) collective-permute-start(f32[256,512]{1,0:T(8,128)} %collective-permute-done.10), channel_id=1, source_target_pairs={{0,1},{1,0},{2,3},{3,2},{4,5},{5,4},{6,7},{7,6},{8,9},{9,8},{10,11... | collective-permute-start | bytes 1572872 | tf_op jit(solution)/shard_map/ppermute | solution.py:20
  155.7 2.0 collective-permute-start.9
  157.2 22.5 %collective-permute-start.19 = (f32[256,512]{1,0:T(8,128)}, f32[256,512]{1,0:T(8,128)S(1)}, u32[]{:S(2)}, u32[]{:S(2)}) collective-permute-start(f32[256,512]{1,0:T(8,128)} %collective-permute-done.18), channel_id=1, source_target_pairs={{0,1},{1,0},{2,3},{3,2},{4,5},{5,4},{6,7},{7,6},{8,9},{9,8},{10,11... | collective-permute-start | bytes 1572872 | tf_op jit(solution)/shard_map/ppermute | solution.py:20
  160.2 7.6 %collective-permute-start.12 = (f32[256,128]{1,0:T(8,128)S(1)}, f32[256,128]{1,0:T(8,128)S(1)}, u32[]{:S(2)}, u32[]{:S(2)}) collective-permute-start(f32[256,128]{1,0:T(8,128)S(1)} %fusion.44), channel_id=1, source_target_pairs={{0,16},{2,18},{4,20},{6,22},{8,24},{10,26},{12,28},{14,30},{1,17},... | collective-permute-start | bytes 393224 | tf_op jit(solution)/shard_map/ppermute | solution.py:13
  167.8 2.3 collective-permute-start.13
  170.1 16.8 %copy-start.2 = (f32[12,512,128]{2,1,0:T(8,128)S(1)}, f32[12,512,128]{2,1,0:T(8,128)}, u32[]{:S(2)}) copy-start(f32[12,512,128]{2,1,0:T(8,128)} %all-gather.2.cloned.1.call-done) | copy-start | bytes 9437188
  170.1 16.8 %copy-start.51 = (f32[1,512]{1,0:T(1,128)S(1)}, f32[1,512]{1,0:T(1,128)}, u32[]{:S(2)}) copy-start(f32[1,512]{1,0:T(1,128)} %copy-done.50) | copy-start | bytes 6148
  170.1 16.8 %copy-start.63 = (f32[512]{0:T(512)S(1)}, f32[512]{0:T(512)}, u32[]{:S(2)}) copy-start(f32[512]{0:T(512)} %broadcast_subtract_fusion.12) | copy-start | bytes 6148
  170.7 11.5 %collective-permute-start.14 = (f32[256,128]{1,0:T(8,128)S(1)}, f32[256,128]{1,0:T(8,128)S(1)}, u32[]{:S(2)}, u32[]{:S(2)}) collective-permute-start(f32[256,128]{1,0:T(8,128)S(1)} %fusion.43), channel_id=1, source_target_pairs={{0,2},{2,4},{4,6},{6,8},{8,10},{10,12},{12,14},{14,16},{16,18},{18... | collective-permute-start | bytes 393224 | tf_op jit(solution)/shard_map/ppermute | solution.py:13
  180.8 8.6 %copy-start.49 = (f32[1,512]{1,0:T(1,128)S(1)}, f32[1,512]{1,0:T(1,128)}, u32[]{:S(2)}) copy-start(f32[1,512]{1,0:T(1,128)} %copy-done.48) | copy-start | bytes 6148
  180.8 8.6 %copy-start.62 = (f32[512]{0:T(512)S(1)}, f32[512]{0:T(512)}, u32[]{:S(2)}) copy-start(f32[512]{0:T(512)} %broadcast_subtract_fusion.11) | copy-start | bytes 6148
  182.2 4.6 %collective-permute-start.15 = (f32[256,128]{1,0:T(8,128)S(1)}, f32[256,128]{1,0:T(8,128)S(1)}, u32[]{:S(2)}, u32[]{:S(2)}) collective-permute-start(f32[256,128]{1,0:T(8,128)S(1)} %broadcast_select_fusion.14), channel_id=1, source_target_pairs={{0,1},{1,0},{2,3},{3,2},{4,5},{5,4},{6,7},{7,6},{8,9},{9,8},{10,11... | collective-permute-start | bytes 393224 | tf_op jit(solution)/shard_map/ppermute | solution.py:20
  184.5 57.0 %collective-permute-start.22 = (f32[256,512]{1,0:T(8,128)S(1)}, f32[256,512]{1,0:T(8,128)}, u32[]{:S(2)}, u32[]{:S(2)}) collective-permute-start(f32[256,512]{1,0:T(8,128)S(1)} %convolution_select_fusion.2), channel_id=1, source_target_pairs={{4,0},{6,2},{8,4},{10,6},{12,8},{14,10},{16,12},{18,14},{20,16},{2... | collective-permute-start | bytes 1572872 | tf_op jit(solution)/shard_map/ppermute | solution.py:13
  199.5 7.7 %copy-start.37 = (f32[1,512]{1,0:T(1,128)S(1)}, f32[1,512]{1,0:T(1,128)}, u32[]{:S(2)}) copy-start(f32[1,512]{1,0:T(1,128)} %get-tuple-element.81) | copy-start | bytes 6148
  199.5 7.7 %copy-start.58 = (f32[512]{0:T(512)S(1)}, f32[512]{0:T(512)}, u32[]{:S(2)}) copy-start(f32[512]{0:T(512)} %broadcast_subtract_fusion.4) | copy-start | bytes 6148
  202.0 7.7 %copy-start.35 = (f32[1,512]{1,0:T(1,128)S(1)}, f32[1,512]{1,0:T(1,128)}, u32[]{:S(2)}) copy-start(f32[1,512]{1,0:T(1,128)} %get-tuple-element.80) | copy-start | bytes 6148
  202.0 7.7 %copy-start.60 = (f32[512]{0:T(512)S(1)}, f32[512]{0:T(512)}, u32[]{:S(2)}) copy-start(f32[512]{0:T(512)} %broadcast_subtract_fusion.3) | copy-start | bytes 6148
  217.1 8.3 %copy-start.3 = (f32[12,512,128]{2,1,0:T(8,128)}, f32[12,512,128]{2,1,0:T(8,128)S(1)}, u32[]{:S(2)}) copy-start(f32[12,512,128]{2,1,0:T(8,128)S(1)} %get-tuple-element.2) | copy-start | bytes 9437188
  217.1 8.3 %slice-start = ((s8[6291456]{0:T(1024)(128)(4,1)}), s8[4194304]{0:T(1024)(128)(4,1)S(1)}, s32[]{:S(2)}) async-start(s8[6291456]{0:T(1024)(128)(4,1)} %bitcast.477), calls=%async_computation.1 | async-start | bytes 8388608
  231.2 9.8 %collective-permute-start.16 = (f32[256,128]{1,0:T(8,128)S(1)}, f32[256,128]{1,0:T(8,128)S(1)}, u32[]{:S(2)}, u32[]{:S(2)}) collective-permute-start(f32[256,128]{1,0:T(8,128)S(1)} %fusion.42), channel_id=1, source_target_pairs={{2,0},{4,2},{6,4},{8,6},{10,8},{12,10},{14,12},{16,14},{18,16},{20... | collective-permute-start | bytes 393224 | tf_op jit(solution)/shard_map/ppermute | solution.py:13
  241.0 1.6 collective-permute-start.17
  241.5 3.5 %collective-permute-start.23 = (f32[256,512]{1,0:T(8,128)}, f32[256,512]{1,0:T(8,128)S(1)}, u32[]{:S(2)}, u32[]{:S(2)}) collective-permute-start(f32[256,512]{1,0:T(8,128)} %collective-permute-done.22), channel_id=1, source_target_pairs={{0,1},{1,0},{2,3},{3,2},{4,5},{5,4},{6,7},{7,6},{8,9},{9,8},{10,11... | collective-permute-start | bytes 1572872 | tf_op jit(solution)/shard_map/ppermute | solution.py:20
  243.1 7.5 %collective-permute-start.20 = (f32[256,128]{1,0:T(8,128)S(1)}, f32[256,128]{1,0:T(8,128)S(1)}, u32[]{:S(2)}, u32[]{:S(2)}) collective-permute-start(f32[256,128]{1,0:T(8,128)S(1)} %fusion.41), channel_id=1, source_target_pairs={{4,0},{6,2},{8,4},{10,6},{12,8},{14,10},{16,12},{18,14},{20,16},{2... | collective-permute-start | bytes 393224 | tf_op jit(solution)/shard_map/ppermute | solution.py:13
  250.6 3.6 %collective-permute-start.21 = (f32[256,128]{1,0:T(8,128)S(1)}, f32[256,128]{1,0:T(8,128)S(1)}, u32[]{:S(2)}, u32[]{:S(2)}) collective-permute-start(f32[256,128]{1,0:T(8,128)S(1)} %collective-permute-done.20), channel_id=1, source_target_pairs={{0,1},{1,0},{2,3},{3,2},{4,5},{5,4},{6,7},{7,6},{8,9},{9,8},{10,11... | collective-permute-start | bytes 393224 | tf_op jit(solution)/shard_map/ppermute | solution.py:20
  252.9 19.0 %collective-permute-start.26 = (f32[256,512]{1,0:T(8,128)S(1)}, f32[256,512]{1,0:T(8,128)S(1)}, u32[]{:S(2)}, u32[]{:S(2)}) collective-permute-start(f32[256,512]{1,0:T(8,128)S(1)} %convolution_select_fusion.1), channel_id=1, source_target_pairs={{8,0},{10,2},{12,4},{14,6},{16,8},{18,10},{20,12},{22,14},{24,16},... | collective-permute-start | bytes 1572872 | tf_op jit(solution)/shard_map/ppermute | solution.py:13
  254.8 16.3 %collective-permute-start.24 = (f32[256,128]{1,0:T(8,128)S(1)}, f32[256,128]{1,0:T(8,128)S(1)}, u32[]{:S(2)}, u32[]{:S(2)}) collective-permute-start(f32[256,128]{1,0:T(8,128)S(1)} %fusion.40), channel_id=1, source_target_pairs={{8,0},{10,2},{12,4},{14,6},{16,8},{18,10},{20,12},{22,14},{24,16},... | collective-permute-start | bytes 393224 | tf_op jit(solution)/shard_map/ppermute | solution.py:13
  271.1 1.8 collective-permute-start.25
  271.9 2.9 collective-permute-start.27
  273.5 24.0 %copy-start.53 = (f32[1,512]{1,0:T(1,128)S(1)}, f32[1,512]{1,0:T(1,128)}, u32[]{:S(2)}) copy-start(f32[1,512]{1,0:T(1,128)} %copy-done.52) | copy-start | bytes 6148
  273.6 10.5 %collective-permute-start.28 = (f32[256,128]{1,0:T(8,128)S(1)}, f32[256,128]{1,0:T(8,128)S(1)}, u32[]{:S(2)}, u32[]{:S(2)}) collective-permute-start(f32[256,128]{1,0:T(8,128)S(1)} %fusion.39), channel_id=1, source_target_pairs={{16,0},{18,2},{20,4},{22,6},{24,8},{26,10},{28,12},{30,14},{17,1},... | collective-permute-start | bytes 393224 | tf_op jit(solution)/shard_map/ppermute | solution.py:13
  284.1 2.2 collective-permute-start.29
  285.2 15.1 %copy-start.29 = (f32[1,512]{1,0:T(1,128)S(1)}, f32[1,512]{1,0:T(1,128)}, u32[]{:S(2)}) copy-start(f32[1,512]{1,0:T(1,128)} %copy-done.28) | copy-start | bytes 6148
  286.2 16.5 %copy-start.27 = (f32[1,512]{1,0:T(1,128)S(1)}, f32[1,512]{1,0:T(1,128)}, u32[]{:S(2)}) copy-start(f32[1,512]{1,0:T(1,128)} %copy-done.26) | copy-start | bytes 6148
  286.9 8.5 %collective-permute-start.30 = (f32[256,128]{1,0:T(8,128)S(1)}, f32[256,128]{1,0:T(8,128)S(1)}, u32[]{:S(2)}, u32[]{:S(2)}) collective-permute-start(f32[256,128]{1,0:T(8,128)S(1)} %fusion.38), channel_id=1, source_target_pairs={{2,0},{4,2},{6,4},{8,6},{10,8},{12,10},{14,12},{16,14},{18,16},{20... | collective-permute-start | bytes 393224 | tf_op jit(solution)/shard_map/ppermute | solution.py:13
  289.4 13.4 %copy-start.1 = (f32[12,512,128]{2,1,0:T(8,128)S(1)}, f32[12,512,128]{2,1,0:T(8,128)}, u32[]{:S(2)}) copy-start(f32[12,512,128]{2,1,0:T(8,128)} %copy-done) | copy-start | bytes 9437188
  295.4 9.0 %copy-start.25 = (f32[1,512]{1,0:T(1,128)S(1)}, f32[1,512]{1,0:T(1,128)}, u32[]{:S(2)}) copy-start(f32[1,512]{1,0:T(1,128)} %copy-done.24) | copy-start | bytes 6148
  295.4 2.2 collective-permute-start.31
  (38 other events, 219.8 us)
Sparse Core Ops, SparseCore 0:
  9.5 14.0 all-gather.1
where the time goes:
time: 335 us; the launch traced here: 330 us
  matrix products  149 us (44%)
  starting transfers between devices  62.6 us (19%)
  waiting for transfers between devices  61.7 us (18%)
  other arithmetic  19.5 us (6%)
  local copies, waits for them, and re-layouts  18 us (5%)
  between operations  16.6 us (5%)
    dot_general x65, matrix products, matmul(): jnp.dot(left, right, precision=HIGHEST, preferred_element_type=jnp.float32)  129 us
    ppermute x16, waiting for transfers between devices, passed_along(): return lax.ppermute(block, axis, route)  57.1 us
    ppermute x16, starting transfers between devices, passed_along(): return lax.ppermute(block, axis, route)  48.8 us
    dot_general x2, matrix products, batched(): lax.dot_general(left, right, (((2,), (1,)), ((0,), (0,))), precision=HIGH...  14.2 us
    ppermute x16, starting transfers between devices, rows_whole(): other = lax.ppermute(part, 'rows', [(0, 1), (1, 0)])  13.8 us
    unnamed x159, local copies, waits for them, and re-layouts  13 us
    sub x12, other arithmetic, forward(): fresh = (1.0 - rate_now)[:, None] * image_now + rate_now[:, None] * obs_now  8.31 us
    select_n x16, other arithmetic, rows_whole(): lower = jnp.where(first_half, part, other)  8.26 us
  transfers between devices with their start and end apart: 33, of which 16 were waited for; matrix products, arithmetic and copies ran while one was open for 49% of the time, Pallas kernels for 0%

commit v1 on v0

--- a/solution.py
+++ b/solution.py
@@ -113,7 +113,7 @@
     entry_whole = rows_whole(entry_rows, 0)
 
     back_lead, back_before = lead_chain(
-        identity_rows, smooth_gain, live_slots, lambda x: matmul(x, transposed), False
+        identity_rows, smooth_gain, live_slots, lambda x: right_transposed(x, transition), False
     )
     back_leads = lead_levels(jnp.where(at_last, 0.0, back_lead), -1, devices, time_index)
 
@@ -129,7 +129,7 @@
     )
     terminal = matmul(transition, final_mean)
     image_all = jnp.concatenate([images[1:], terminal[None]], axis=0)
-    pulled = jnp.einsum("ij,tjk->tik", transposed, image_all, precision=HIGHEST,
+    pulled = jnp.einsum("ji,tjk->tik", transition, image_all, precision=HIGHEST,
                         preferred_element_type=jnp.float32)
     offsets = filtered_whole - smooth_gain[:, :, None] * pulled
 

time: 335 us -> 335 us (level)
    dot_general x1 -> x13, matrix products: 6.4 us -> 46.2 us  [the longest x12 39.8 us: right_transposed(): lax.dot_general(left, right, (((1,), (1,)), ((), ())), precision=HIGHEST,...]
    dot_general x65 -> x53, matrix products: 129 us -> 88.9 us  [matmul(): jnp.dot(left, right, precision=HIGHEST, preferred_element_type=jnp.float32)]
where the time goes in v1:
time: 335 us; the launch traced here: 330 us
  matrix products  149 us (44%)
  starting transfers between devices  62.6 us (19%)
  waiting for transfers between devices  61.7 us (18%)
  other arithmetic  19.5 us (6%)
  local copies, waits for them, and re-layouts  18 us (5%)
  between operations  16.6 us (5%)
    dot_general x53, matrix products, matmul(): jnp.dot(left, right, precision=HIGHEST, preferred_element_type=jnp.float32)  88.9 us
    ppermute x16, waiting for transfers between devices, passed_along(): return lax.ppermute(block, axis, route)  57.1 us
    ppermute x16, starting transfers between devices, passed_along(): return lax.ppermute(block, axis, route)  48.8 us
    dot_general x12, matrix products, right_transposed(): lax.dot_general(left, right, (((1,), (1,)), ((), ())), precision=HIGHEST,...  39.8 us
    dot_general x2, matrix products, batched(): lax.dot_general(left, right, (((2,), (1,)), ((0,), (0,))), precision=HIGH...  14.2 us
    ppermute x16, starting transfers between devices, rows_whole(): other = lax.ppermute(part, 'rows', [(0, 1), (1, 0)])  13.8 us
    unnamed x159, local copies, waits for them, and re-layouts  13 us
    sub x12, other arithmetic, forward(): fresh = (1.0 - rate_now)[:, None] * image_now + rate_now[:, None] * obs_now  8.31 us
  transfers between devices with their start and end apart: 33, of which 16 were waited for; matrix products, arithmetic and copies ran while one was open for 49% of the time, Pallas kernels for 0%

profile of v1, /device:TPU:7, one launch (start us, length us, event | category | flops | bytes accessed | tf_op | source)
XLA Modules:
  0.0 329.8 jit_solution(2598821250726902152)
XLA Ops:
  7.9 2.5 copy.10
  13.6 1.7 mul.554
  15.4 1.8 convolution_select_fusion.29
  20.4 1.7 convolution_select_fusion.26
  22.1 1.8 convolution_select_fusion.25
  23.9 1.7 convolution_select_fusion.24
  27.2 1.7 convolution_select_fusion.22
  28.9 1.7 convolution_select_fusion.21
  30.7 1.8 convolution_select_fusion.20
  32.4 2.7 bitcast_dynamic-update-slice_fusion.21
  35.2 2.5 broadcast_select_fusion.1
  37.7 3.1 collective-permute-start.2
  50.5 2.5 bitcast_dynamic-update-slice_fusion.10
  53.0 2.4 bitcast_dynamic-update-slice_fusion.9
  55.4 2.5 bitcast_dynamic-update-slice_fusion.8
  58.0 2.5 bitcast_dynamic-update-slice_fusion.7
  60.5 2.5 bitcast_dynamic-update-slice_fusion.6
  63.0 2.5 bitcast_dynamic-update-slice_fusion.5
  65.5 2.5 bitcast_dynamic-update-slice_fusion.4
  68.0 2.6 bitcast_dynamic-update-slice_fusion.3
  70.5 2.5 bitcast_dynamic-update-slice_fusion.2
  73.0 2.4 bitcast_dynamic-update-slice_fusion.1
  75.4 2.5 bitcast_dynamic-update-slice_fusion
  78.0 12.3 %broadcast_select_fusion = (f32[256,512]{1,0:T(8,128)S(1)}, f32[256,512]{1,0:T(8,128)S(1)}) fusion(pred[]{:T(512)S(6)} %eq.58, f32[256,512]{1,0:T(8,128)S(1)} %get-tuple-element.146, f32[512,512]{0,1:T(8,128)S(1)} %mul.554, f32[512]{0:T(512)S(1)} %bitcast.488, pred[]{:T(512)} %bitcast.13), kind=kOutput, calls=%fused_computation.331 | convolution fusion | flops 805699584 | bytes 2623490 | tf_op jit(solution)/shard_map/eval_jaxpr/dot_general | solution.py:38
  90.3 2.2 collective-permute-start.18
  97.9 2.0 all_gather.7
  104.6 3.2 collective-permute-start.6
  107.9 9.1 %fusion.48 = f32[256,128]{1,0:T(8,128)S(1)} fusion(f32[12,256,512]{2,1,0:T(8,128)} %get-tuple-element.104, f32[12,512,128]{2,1,0:T(8,128)} %all-gather.2.cloned.1.call-done, f32[12,512]{1,0:T(8,128)} %param.8, pred[12]{0:T(512)(128)(4,1)S(1)} %iota_compare_fusion.4), kind=kOutput, calls=%fused_computation.102 | convolution fusion | flops 2417491968 | bytes 9592844 | tf_op jit(solution)/shard_map/dot_general | solution.py:44
  117.5 4.0 %collective-permute-start = (f32[256,128]{1,0:T(8,128)S(1)}, f32[256,128]{1,0:T(8,128)S(1)}, u32[]{:S(2)}, u32[]{:S(2)}) collective-permute-start(f32[256,128]{1,0:T(8,128)S(1)} %fusion.47), channel_id=1, source_target_pairs={{0,2},{2,4},{4,6},{6,8},{8,10},{10,12},{12,14},{14,16},{16,18},{18... | collective-permute-start | bytes 393224 | tf_op jit(solution)/shard_map/ppermute | solution.py:13
  122.9 2.1 collective-permute-done
  129.6 3.4 %collective-permute-start.4 = (f32[256,128]{1,0:T(8,128)S(1)}, f32[256,128]{1,0:T(8,128)S(1)}, u32[]{:S(2)}, u32[]{:S(2)}) collective-permute-start(f32[256,128]{1,0:T(8,128)S(1)} %fusion.46), channel_id=1, source_target_pairs={{0,4},{2,6},{4,8},{6,10},{8,12},{10,14},{12,16},{14,18},{16,20},{1... | collective-permute-start | bytes 393224 | tf_op jit(solution)/shard_map/ppermute | solution.py:13
  134.3 1.9 collective-permute-done.4
  138.4 4.1 %collective-permute-start.10 = (f32[256,512]{1,0:T(8,128)S(1)}, f32[256,512]{1,0:T(8,128)}, u32[]{:S(2)}, u32[]{:S(2)}) collective-permute-start(f32[256,512]{1,0:T(8,128)S(1)} %convolution_select_fusion.4), channel_id=1, source_target_pairs={{0,8},{2,10},{4,12},{6,14},{8,16},{10,18},{12,20},{14,22},{16,24},... | collective-permute-start | bytes 1572872 | tf_op jit(solution)/shard_map/ppermute | solution.py:13
  143.1 2.3 collective-permute-start.8
  146.1 6.8 %collective-permute-done.10 = f32[256,512]{1,0:T(8,128)} collective-permute-done((f32[256,512]{1,0:T(8,128)S(1)}, f32[256,512]{1,0:T(8,128)}, u32[]{:S(2)}, u32[]{:S(2)}) %collective-permute-start.10) | collective-permute-done | bytes 524320 | tf_op jit(solution)/shard_map/ppermute | solution.py:13
  160.2 5.1 %collective-permute-start.12 = (f32[256,128]{1,0:T(8,128)S(1)}, f32[256,128]{1,0:T(8,128)S(1)}, u32[]{:S(2)}, u32[]{:S(2)}) collective-permute-start(f32[256,128]{1,0:T(8,128)S(1)} %fusion.44), channel_id=1, source_target_pairs={{0,16},{2,18},{4,20},{6,22},{8,24},{10,26},{12,28},{14,30},{1,17},... | collective-permute-start | bytes 393224 | tf_op jit(solution)/shard_map/ppermute | solution.py:13
  170.7 8.9 %collective-permute-start.14 = (f32[256,128]{1,0:T(8,128)S(1)}, f32[256,128]{1,0:T(8,128)S(1)}, u32[]{:S(2)}, u32[]{:S(2)}) collective-permute-start(f32[256,128]{1,0:T(8,128)S(1)} %fusion.43), channel_id=1, source_target_pairs={{0,2},{2,4},{4,6},{6,8},{8,10},{10,12},{12,14},{14,16},{16,18},{18... | collective-permute-start | bytes 393224 | tf_op jit(solution)/shard_map/ppermute | solution.py:13
  184.5 2.3 collective-permute-start.22
  186.9 2.5 bitcast_dynamic-update-slice_fusion.56
  189.4 2.4 bitcast_dynamic-update-slice_fusion.55
  191.9 2.5 bitcast_dynamic-update-slice_fusion.54
  194.5 2.5 bitcast_dynamic-update-slice_fusion.53
  197.0 2.5 bitcast_dynamic-update-slice_fusion.52
  199.5 2.4 bitcast_dynamic-update-slice_fusion.51
  202.0 2.6 bitcast_dynamic-update-slice_fusion.50
  204.7 2.5 bitcast_dynamic-update-slice_fusion.49
  207.2 2.5 bitcast_dynamic-update-slice_fusion.48
  209.7 2.4 bitcast_dynamic-update-slice_fusion.47
  212.1 2.4 bitcast_dynamic-update-slice_fusion.46
  214.6 2.5 bitcast_dynamic-update-slice_fusion.45
  217.2 1.8 bitcast_dynamic-update-slice_fusion.33
  219.0 6.4 %bitcast_subtract_fusion = f32[12,512,128]{2,1,0:T(8,128)S(1)} fusion(f32[12,512,128]{2,1,0:T(8,128)S(1)} %get-tuple-element.2, f32[12,512,128]{2,1,0:T(8,128)S(1)} %get-tuple-element.123, f32[12,512]{1,0:T(8,128)S(1)} %copy-done.13, f32[512,512]{0,1:T(8,128)S(1)} %mul.554), kind=kOutput, calls=%fused_computation | convolution fusion | flops 4833411072 | bytes 10510336 | tf_op jit(solution)/shard_map/ji,tjk->tik/dot_general | solution.py:132
  225.4 5.1 %fusion.51 = f32[256,128]{1,0:T(8,128)S(1)} fusion(f32[12,256,512]{2,1,0:T(8,128)S(1)} %bitcast.441, f32[12,512,128]{2,1,0:T(8,128)S(1)} %bitcast_subtract_fusion, pred[12]{0:T(512)(128)(4,1)S(1)} %iota_compare_fusion.4), kind=kOutput, calls=%fused_computation.103 | convolution fusion | flops 2416705536 | bytes 9568268 | tf_op jit(solution)/shard_map/dot_general | solution.py:44
  231.2 1.9 collective-permute-start.16
  233.1 7.8 %collective-permute-done.16 = f32[256,128]{1,0:T(8,128)S(1)} collective-permute-done((f32[256,128]{1,0:T(8,128)S(1)}, f32[256,128]{1,0:T(8,128)S(1)}, u32[]{:S(2)}, u32[]{:S(2)}) %collective-permute-start.16) | collective-permute-done | bytes 131104 | tf_op jit(solution)/shard_map/ppermute | solution.py:13
  243.1 1.9 collective-permute-start.20
  246.2 4.4 %collective-permute-done.20 = f32[256,128]{1,0:T(8,128)S(1)} collective-permute-done((f32[256,128]{1,0:T(8,128)S(1)}, f32[256,128]{1,0:T(8,128)S(1)}, u32[]{:S(2)}, u32[]{:S(2)}) %collective-permute-start.20) | collective-permute-done | bytes 131104 | tf_op jit(solution)/shard_map/ppermute | solution.py:13
  256.1 15.0 %collective-permute-done.24 = f32[256,128]{1,0:T(8,128)S(1)} collective-permute-done((f32[256,128]{1,0:T(8,128)S(1)}, f32[256,128]{1,0:T(8,128)S(1)}, u32[]{:S(2)}, u32[]{:S(2)}) %collective-permute-start.24) | collective-permute-done | bytes 131104 | tf_op jit(solution)/shard_map/ppermute | solution.py:13
  275.0 9.1 %collective-permute-done.28 = f32[256,128]{1,0:T(8,128)S(1)} collective-permute-done((f32[256,128]{1,0:T(8,128)S(1)}, f32[256,128]{1,0:T(8,128)S(1)}, u32[]{:S(2)}, u32[]{:S(2)}) %collective-permute-start.28) | collective-permute-done | bytes 131104 | tf_op jit(solution)/shard_map/ppermute | solution.py:13
  286.9 2.5 collective-permute-start.30
  289.4 5.9 %collective-permute-done.30 = f32[256,128]{1,0:T(8,128)S(1)} collective-permute-done((f32[256,128]{1,0:T(8,128)S(1)}, f32[256,128]{1,0:T(8,128)S(1)}, u32[]{:S(2)}, u32[]{:S(2)}) %collective-permute-start.30) | collective-permute-done | bytes 131104 | tf_op jit(solution)/shard_map/ppermute | solution.py:13
  297.6 2.6 fusion.35
  300.2 2.5 fusion.33
  320.9 1.9 constant_dynamic-slice_fusion
  (277 shorter events, 92.7 us)
Async XLA Ops:
  7.2 100.6 %all-gather.2.cloned.1.call-start = ((), (), s32[]{:S(2)}) async-start(), calls=%async_computation | async-start | bytes 4718592 | tf_op jit(solution)/shard_map/all_gather | solution.py:100
  37.7 58.4 %collective-permute-start.2 = (f32[256,512]{1,0:T(8,128)S(1)}, f32[256,512]{1,0:T(8,128)S(1)}, u32[]{:S(2)}, u32[]{:S(2)}) collective-permute-start(f32[256,512]{1,0:T(8,128)S(1)} %get-tuple-element.119), channel_id=1, source_target_pairs={{0,2},{2,4},{4,6},{6,8},{8,10},{10,12},{12,14},{14,16},{16,18},{18... | collective-permute-start | bytes 1572872 | tf_op jit(solution)/shard_map/ppermute | solution.py:13
  50.4 10.1 %copy-start.16 = (f32[1,512]{1,0:T(1,128)}, f32[1,512]{1,0:T(1,128)S(1)}, u32[]{:S(2)}) copy-start(f32[1,512]{1,0:T(1,128)S(1)} %get-tuple-element.74) | copy-start | bytes 6148
  50.4 12.6 %copy-start.18 = (f32[1,512]{1,0:T(1,128)}, f32[1,512]{1,0:T(1,128)S(1)}, u32[]{:S(2)}) copy-start(f32[1,512]{1,0:T(1,128)S(1)} %get-tuple-element.73) | copy-start | bytes 6148
  50.4 15.0 %copy-start.20 = (f32[1,512]{1,0:T(1,128)}, f32[1,512]{1,0:T(1,128)S(1)}, u32[]{:S(2)}) copy-start(f32[1,512]{1,0:T(1,128)S(1)} %get-tuple-element.72) | copy-start | bytes 6148
  50.4 17.5 %copy-start.22 = (f32[1,512]{1,0:T(1,128)}, f32[1,512]{1,0:T(1,128)S(1)}, u32[]{:S(2)}) copy-start(f32[1,512]{1,0:T(1,128)S(1)} %get-tuple-element.71) | copy-start | bytes 6148
  50.4 20.1 %copy-start.24 = (f32[1,512]{1,0:T(1,128)}, f32[1,512]{1,0:T(1,128)S(1)}, u32[]{:S(2)}) copy-start(f32[1,512]{1,0:T(1,128)S(1)} %get-tuple-element.70) | copy-start | bytes 6148
  50.4 22.6 %copy-start.26 = (f32[1,512]{1,0:T(1,128)}, f32[1,512]{1,0:T(1,128)S(1)}, u32[]{:S(2)}) copy-start(f32[1,512]{1,0:T(1,128)S(1)} %get-tuple-element.69) | copy-start | bytes 6148
  50.4 25.0 %copy-start.28 = (f32[1,512]{1,0:T(1,128)}, f32[1,512]{1,0:T(1,128)S(1)}, u32[]{:S(2)}) copy-start(f32[1,512]{1,0:T(1,128)S(1)} %get-tuple-element.68) | copy-start | bytes 6148
  50.5 27.5 %copy-start.52 = (f32[1,512]{1,0:T(1,128)}, f32[1,512]{1,0:T(1,128)S(1)}, u32[]{:S(2)}) copy-start(f32[1,512]{1,0:T(1,128)S(1)} %get-tuple-element.67) | copy-start | bytes 6148
  75.4 22.5 %copy-start.6 = (f32[256,128]{1,0:T(8,128)S(1)}, f32[256,128]{1,0:T(8,128)}, u32[]{:S(2)}) copy-start(f32[256,128]{1,0:T(8,128)} %param.12) | copy-start | bytes 393220
  90.3 66.8 %collective-permute-start.18 = (f32[256,512]{1,0:T(8,128)S(1)}, f32[256,512]{1,0:T(8,128)}, u32[]{:S(2)}, u32[]{:S(2)}) collective-permute-start(f32[256,512]{1,0:T(8,128)S(1)} %get-tuple-element.147), channel_id=1, source_target_pairs={{2,0},{4,2},{6,4},{8,6},{10,8},{12,10},{14,12},{16,14},{18,16},{20... | collective-permute-start | bytes 1572872 | tf_op jit(solution)/shard_map/ppermute | solution.py:13
  96.1 6.4 %collective-permute-start.3 = (f32[256,512]{1,0:T(8,128)S(1)}, f32[256,512]{1,0:T(8,128)}, u32[]{:S(2)}, u32[]{:S(2)}) collective-permute-start(f32[256,512]{1,0:T(8,128)S(1)} %collective-permute-done.2), channel_id=1, source_target_pairs={{0,1},{1,0},{2,3},{3,2},{4,5},{5,4},{6,7},{7,6},{8,9},{9,8},{10,11... | collective-permute-start | bytes 1572872 | tf_op jit(solution)/shard_map/ppermute | solution.py:20
  104.6 17.5 %collective-permute-start.6 = (f32[256,512]{1,0:T(8,128)S(1)}, f32[256,512]{1,0:T(8,128)}, u32[]{:S(2)}, u32[]{:S(2)}) collective-permute-start(f32[256,512]{1,0:T(8,128)S(1)} %convolution_select_fusion.5), channel_id=1, source_target_pairs={{0,4},{2,6},{4,8},{6,10},{8,12},{10,14},{12,16},{14,18},{16,20},{1... | collective-permute-start | bytes 1572872 | tf_op jit(solution)/shard_map/ppermute | solution.py:13
  107.8 9.1 %copy-start.5 = (f32[256,512]{1,0:T(8,128)S(1)}, f32[256,512]{1,0:T(8,128)}, u32[]{:S(2)}) copy-start(f32[256,512]{1,0:T(8,128)} %get-tuple-element.120) | copy-start | bytes 1572868
  107.8 13.7 %copy-start.36 = (f32[1,512]{1,0:T(1,128)S(1)}, f32[1,512]{1,0:T(1,128)}, u32[]{:S(2)}) copy-start(f32[1,512]{1,0:T(1,128)} %get-tuple-element.81) | copy-start | bytes 6148
  107.8 18.1 %copy-start.34 = (f32[1,512]{1,0:T(1,128)S(1)}, f32[1,512]{1,0:T(1,128)}, u32[]{:S(2)}) copy-start(f32[1,512]{1,0:T(1,128)} %get-tuple-element.80) | copy-start | bytes 6148
  117.5 7.4 %collective-permute-start = (f32[256,128]{1,0:T(8,128)S(1)}, f32[256,128]{1,0:T(8,128)S(1)}, u32[]{:S(2)}, u32[]{:S(2)}) collective-permute-start(f32[256,128]{1,0:T(8,128)S(1)} %fusion.47), channel_id=1, source_target_pairs={{0,2},{2,4},{4,6},{6,8},{8,10},{10,12},{12,14},{14,16},{16,18},{18... | collective-permute-start | bytes 393224 | tf_op jit(solution)/shard_map/ppermute | solution.py:13
  122.1 10.8 %collective-permute-start.7 = (f32[256,512]{1,0:T(8,128)}, f32[256,512]{1,0:T(8,128)}, u32[]{:S(2)}, u32[]{:S(2)}) collective-permute-start(f32[256,512]{1,0:T(8,128)} %collective-permute-done.6), channel_id=1, source_target_pairs={{0,1},{1,0},{2,3},{3,2},{4,5},{5,4},{6,7},{7,6},{8,9},{9,8},{10,11... | collective-permute-start | bytes 1572872 | tf_op jit(solution)/shard_map/ppermute | solution.py:20
  124.9 2.1 collective-permute-start.1
  129.5 15.9 %copy-start.32 = (f32[1,512]{1,0:T(1,128)S(1)}, f32[1,512]{1,0:T(1,128)}, u32[]{:S(2)}) copy-start(f32[1,512]{1,0:T(1,128)} %get-tuple-element.90) | copy-start | bytes 6148
  129.5 27.0 %copy-start.30 = (f32[1,512]{1,0:T(1,128)S(1)}, f32[1,512]{1,0:T(1,128)}, u32[]{:S(2)}) copy-start(f32[1,512]{1,0:T(1,128)} %get-tuple-element.79) | copy-start | bytes 6148
  129.6 6.6 %collective-permute-start.4 = (f32[256,128]{1,0:T(8,128)S(1)}, f32[256,128]{1,0:T(8,128)S(1)}, u32[]{:S(2)}, u32[]{:S(2)}) collective-permute-start(f32[256,128]{1,0:T(8,128)S(1)} %fusion.46), channel_id=1, source_target_pairs={{0,4},{2,6},{4,8},{6,10},{8,12},{10,14},{12,16},{14,18},{16,20},{1... | collective-permute-start | bytes 393224 | tf_op jit(solution)/shard_map/ppermute | solution.py:13
  136.1 6.4 %collective-permute-start.5 = (f32[256,128]{1,0:T(8,128)S(1)}, f32[256,128]{1,0:T(8,128)S(1)}, u32[]{:S(2)}, u32[]{:S(2)}) collective-permute-start(f32[256,128]{1,0:T(8,128)S(1)} %collective-permute-done.4), channel_id=1, source_target_pairs={{0,1},{1,0},{2,3},{3,2},{4,5},{5,4},{6,7},{7,6},{8,9},{9,8},{10,11... | collective-permute-start | bytes 393224 | tf_op jit(solution)/shard_map/ppermute | solution.py:20
  138.4 14.5 %collective-permute-start.10 = (f32[256,512]{1,0:T(8,128)S(1)}, f32[256,512]{1,0:T(8,128)}, u32[]{:S(2)}, u32[]{:S(2)}) collective-permute-start(f32[256,512]{1,0:T(8,128)S(1)} %convolution_select_fusion.4), channel_id=1, source_target_pairs={{0,8},{2,10},{4,12},{6,14},{8,16},{10,18},{12,20},{14,22},{16,24},... | collective-permute-start | bytes 1572872 | tf_op jit(solution)/shard_map/ppermute | solution.py:13
  143.1 9.8 %copy-start.7 = (f32[256,128]{1,0:T(8,128)}, f32[256,128]{1,0:T(8,128)S(1)}, u32[]{:S(2)}) copy-start(f32[256,128]{1,0:T(8,128)S(1)} %fusion.45) | copy-start | bytes 393220
  143.1 12.6 %collective-permute-start.8 = (f32[256,128]{1,0:T(8,128)S(1)}, f32[256,128]{1,0:T(8,128)S(1)}, u32[]{:S(2)}, u32[]{:S(2)}) collective-permute-start(f32[256,128]{1,0:T(8,128)S(1)} %fusion.45), channel_id=1, source_target_pairs={{0,8},{2,10},{4,12},{6,14},{8,16},{10,18},{12,20},{14,22},{16,24},... | collective-permute-start | bytes 393224 | tf_op jit(solution)/shard_map/ppermute | solution.py:13
  152.9 12.4 %collective-permute-start.11 = (f32[256,512]{1,0:T(8,128)}, f32[256,512]{1,0:T(8,128)}, u32[]{:S(2)}, u32[]{:S(2)}) collective-permute-start(f32[256,512]{1,0:T(8,128)} %collective-permute-done.10), channel_id=1, source_target_pairs={{0,1},{1,0},{2,3},{3,2},{4,5},{5,4},{6,7},{7,6},{8,9},{9,8},{10,11... | collective-permute-start | bytes 1572872 | tf_op jit(solution)/shard_map/ppermute | solution.py:20
  155.7 2.0 collective-permute-start.9
  157.2 22.5 %collective-permute-start.19 = (f32[256,512]{1,0:T(8,128)}, f32[256,512]{1,0:T(8,128)S(1)}, u32[]{:S(2)}, u32[]{:S(2)}) collective-permute-start(f32[256,512]{1,0:T(8,128)} %collective-permute-done.18), channel_id=1, source_target_pairs={{0,1},{1,0},{2,3},{3,2},{4,5},{5,4},{6,7},{7,6},{8,9},{9,8},{10,11... | collective-permute-start | bytes 1572872 | tf_op jit(solution)/shard_map/ppermute | solution.py:20
  160.2 7.6 %collective-permute-start.12 = (f32[256,128]{1,0:T(8,128)S(1)}, f32[256,128]{1,0:T(8,128)S(1)}, u32[]{:S(2)}, u32[]{:S(2)}) collective-permute-start(f32[256,128]{1,0:T(8,128)S(1)} %fusion.44), channel_id=1, source_target_pairs={{0,16},{2,18},{4,20},{6,22},{8,24},{10,26},{12,28},{14,30},{1,17},... | collective-permute-start | bytes 393224 | tf_op jit(solution)/shard_map/ppermute | solution.py:13
  167.8 2.3 collective-permute-start.13
  170.1 16.8 %copy-start.2 = (f32[12,512,128]{2,1,0:T(8,128)S(1)}, f32[12,512,128]{2,1,0:T(8,128)}, u32[]{:S(2)}) copy-start(f32[12,512,128]{2,1,0:T(8,128)} %all-gather.2.cloned.1.call-done) | copy-start | bytes 9437188
  170.1 16.8 %copy-start.51 = (f32[1,512]{1,0:T(1,128)S(1)}, f32[1,512]{1,0:T(1,128)}, u32[]{:S(2)}) copy-start(f32[1,512]{1,0:T(1,128)} %copy-done.50) | copy-start | bytes 6148
  170.1 16.8 %copy-start.63 = (f32[512]{0:T(512)S(1)}, f32[512]{0:T(512)}, u32[]{:S(2)}) copy-start(f32[512]{0:T(512)} %broadcast_subtract_fusion.12) | copy-start | bytes 6148
  170.7 11.5 %collective-permute-start.14 = (f32[256,128]{1,0:T(8,128)S(1)}, f32[256,128]{1,0:T(8,128)S(1)}, u32[]{:S(2)}, u32[]{:S(2)}) collective-permute-start(f32[256,128]{1,0:T(8,128)S(1)} %fusion.43), channel_id=1, source_target_pairs={{0,2},{2,4},{4,6},{6,8},{8,10},{10,12},{12,14},{14,16},{16,18},{18... | collective-permute-start | bytes 393224 | tf_op jit(solution)/shard_map/ppermute | solution.py:13
  180.8 8.6 %copy-start.49 = (f32[1,512]{1,0:T(1,128)S(1)}, f32[1,512]{1,0:T(1,128)}, u32[]{:S(2)}) copy-start(f32[1,512]{1,0:T(1,128)} %copy-done.48) | copy-start | bytes 6148
  180.8 8.6 %copy-start.62 = (f32[512]{0:T(512)S(1)}, f32[512]{0:T(512)}, u32[]{:S(2)}) copy-start(f32[512]{0:T(512)} %broadcast_subtract_fusion.11) | copy-start | bytes 6148
  182.2 4.6 %collective-permute-start.15 = (f32[256,128]{1,0:T(8,128)S(1)}, f32[256,128]{1,0:T(8,128)S(1)}, u32[]{:S(2)}, u32[]{:S(2)}) collective-permute-start(f32[256,128]{1,0:T(8,128)S(1)} %broadcast_select_fusion.14), channel_id=1, source_target_pairs={{0,1},{1,0},{2,3},{3,2},{4,5},{5,4},{6,7},{7,6},{8,9},{9,8},{10,11... | collective-permute-start | bytes 393224 | tf_op jit(solution)/shard_map/ppermute | solution.py:20
  184.5 57.0 %collective-permute-start.22 = (f32[256,512]{1,0:T(8,128)S(1)}, f32[256,512]{1,0:T(8,128)}, u32[]{:S(2)}, u32[]{:S(2)}) collective-permute-start(f32[256,512]{1,0:T(8,128)S(1)} %convolution_select_fusion.2), channel_id=1, source_target_pairs={{4,0},{6,2},{8,4},{10,6},{12,8},{14,10},{16,12},{18,14},{20,16},{2... | collective-permute-start | bytes 1572872 | tf_op jit(solution)/shard_map/ppermute | solution.py:13
  199.5 7.7 %copy-start.37 = (f32[1,512]{1,0:T(1,128)S(1)}, f32[1,512]{1,0:T(1,128)}, u32[]{:S(2)}) copy-start(f32[1,512]{1,0:T(1,128)} %get-tuple-element.81) | copy-start | bytes 6148
  199.5 7.7 %copy-start.58 = (f32[512]{0:T(512)S(1)}, f32[512]{0:T(512)}, u32[]{:S(2)}) copy-start(f32[512]{0:T(512)} %broadcast_subtract_fusion.4) | copy-start | bytes 6148
  202.0 7.7 %copy-start.35 = (f32[1,512]{1,0:T(1,128)S(1)}, f32[1,512]{1,0:T(1,128)}, u32[]{:S(2)}) copy-start(f32[1,512]{1,0:T(1,128)} %get-tuple-element.80) | copy-start | bytes 6148
  202.0 7.7 %copy-start.60 = (f32[512]{0:T(512)S(1)}, f32[512]{0:T(512)}, u32[]{:S(2)}) copy-start(f32[512]{0:T(512)} %broadcast_subtract_fusion.3) | copy-start | bytes 6148
  217.1 8.3 %copy-start.3 = (f32[12,512,128]{2,1,0:T(8,128)}, f32[12,512,128]{2,1,0:T(8,128)S(1)}, u32[]{:S(2)}) copy-start(f32[12,512,128]{2,1,0:T(8,128)S(1)} %get-tuple-element.2) | copy-start | bytes 9437188
  217.1 8.3 %slice-start = ((s8[6291456]{0:T(1024)(128)(4,1)}), s8[4194304]{0:T(1024)(128)(4,1)S(1)}, s32[]{:S(2)}) async-start(s8[6291456]{0:T(1024)(128)(4,1)} %bitcast.440), calls=%async_computation.1 | async-start | bytes 8388608
  231.2 9.8 %collective-permute-start.16 = (f32[256,128]{1,0:T(8,128)S(1)}, f32[256,128]{1,0:T(8,128)S(1)}, u32[]{:S(2)}, u32[]{:S(2)}) collective-permute-start(f32[256,128]{1,0:T(8,128)S(1)} %fusion.42), channel_id=1, source_target_pairs={{2,0},{4,2},{6,4},{8,6},{10,8},{12,10},{14,12},{16,14},{18,16},{20... | collective-permute-start | bytes 393224 | tf_op jit(solution)/shard_map/ppermute | solution.py:13
  241.0 1.6 collective-permute-start.17
  241.5 3.5 %collective-permute-start.23 = (f32[256,512]{1,0:T(8,128)}, f32[256,512]{1,0:T(8,128)S(1)}, u32[]{:S(2)}, u32[]{:S(2)}) collective-permute-start(f32[256,512]{1,0:T(8,128)} %collective-permute-done.22), channel_id=1, source_target_pairs={{0,1},{1,0},{2,3},{3,2},{4,5},{5,4},{6,7},{7,6},{8,9},{9,8},{10,11... | collective-permute-start | bytes 1572872 | tf_op jit(solution)/shard_map/ppermute | solution.py:20
  243.1 7.5 %collective-permute-start.20 = (f32[256,128]{1,0:T(8,128)S(1)}, f32[256,128]{1,0:T(8,128)S(1)}, u32[]{:S(2)}, u32[]{:S(2)}) collective-permute-start(f32[256,128]{1,0:T(8,128)S(1)} %fusion.41), channel_id=1, source_target_pairs={{4,0},{6,2},{8,4},{10,6},{12,8},{14,10},{16,12},{18,14},{20,16},{2... | collective-permute-start | bytes 393224 | tf_op jit(solution)/shard_map/ppermute | solution.py:13
  250.6 3.6 %collective-permute-start.21 = (f32[256,128]{1,0:T(8,128)S(1)}, f32[256,128]{1,0:T(8,128)S(1)}, u32[]{:S(2)}, u32[]{:S(2)}) collective-permute-start(f32[256,128]{1,0:T(8,128)S(1)} %collective-permute-done.20), channel_id=1, source_target_pairs={{0,1},{1,0},{2,3},{3,2},{4,5},{5,4},{6,7},{7,6},{8,9},{9,8},{10,11... | collective-permute-start | bytes 393224 | tf_op jit(solution)/shard_map/ppermute | solution.py:20
  252.9 19.0 %collective-permute-start.26 = (f32[256,512]{1,0:T(8,128)S(1)}, f32[256,512]{1,0:T(8,128)S(1)}, u32[]{:S(2)}, u32[]{:S(2)}) collective-permute-start(f32[256,512]{1,0:T(8,128)S(1)} %convolution_select_fusion.1), channel_id=1, source_target_pairs={{8,0},{10,2},{12,4},{14,6},{16,8},{18,10},{20,12},{22,14},{24,16},... | collective-permute-start | bytes 1572872 | tf_op jit(solution)/shard_map/ppermute | solution.py:13
  254.8 16.3 %collective-permute-start.24 = (f32[256,128]{1,0:T(8,128)S(1)}, f32[256,128]{1,0:T(8,128)S(1)}, u32[]{:S(2)}, u32[]{:S(2)}) collective-permute-start(f32[256,128]{1,0:T(8,128)S(1)} %fusion.40), channel_id=1, source_target_pairs={{8,0},{10,2},{12,4},{14,6},{16,8},{18,10},{20,12},{22,14},{24,16},... | collective-permute-start | bytes 393224 | tf_op jit(solution)/shard_map/ppermute | solution.py:13
  271.1 1.8 collective-permute-start.25
  271.9 2.9 collective-permute-start.27
  273.5 24.0 %copy-start.53 = (f32[1,512]{1,0:T(1,128)S(1)}, f32[1,512]{1,0:T(1,128)}, u32[]{:S(2)}) copy-start(f32[1,512]{1,0:T(1,128)} %copy-done.52) | copy-start | bytes 6148
  273.6 10.5 %collective-permute-start.28 = (f32[256,128]{1,0:T(8,128)S(1)}, f32[256,128]{1,0:T(8,128)S(1)}, u32[]{:S(2)}, u32[]{:S(2)}) collective-permute-start(f32[256,128]{1,0:T(8,128)S(1)} %fusion.39), channel_id=1, source_target_pairs={{16,0},{18,2},{20,4},{22,6},{24,8},{26,10},{28,12},{30,14},{17,1},... | collective-permute-start | bytes 393224 | tf_op jit(solution)/shard_map/ppermute | solution.py:13
  284.1 2.2 collective-permute-start.29
  285.2 15.1 %copy-start.29 = (f32[1,512]{1,0:T(1,128)S(1)}, f32[1,512]{1,0:T(1,128)}, u32[]{:S(2)}) copy-start(f32[1,512]{1,0:T(1,128)} %copy-done.28) | copy-start | bytes 6148
  286.2 16.5 %copy-start.27 = (f32[1,512]{1,0:T(1,128)S(1)}, f32[1,512]{1,0:T(1,128)}, u32[]{:S(2)}) copy-start(f32[1,512]{1,0:T(1,128)} %copy-done.26) | copy-start | bytes 6148
  286.9 8.5 %collective-permute-start.30 = (f32[256,128]{1,0:T(8,128)S(1)}, f32[256,128]{1,0:T(8,128)S(1)}, u32[]{:S(2)}, u32[]{:S(2)}) collective-permute-start(f32[256,128]{1,0:T(8,128)S(1)} %fusion.38), channel_id=1, source_target_pairs={{2,0},{4,2},{6,4},{8,6},{10,8},{12,10},{14,12},{16,14},{18,16},{20... | collective-permute-start | bytes 393224 | tf_op jit(solution)/shard_map/ppermute | solution.py:13
  289.4 13.4 %copy-start.1 = (f32[12,512,128]{2,1,0:T(8,128)S(1)}, f32[12,512,128]{2,1,0:T(8,128)}, u32[]{:S(2)}) copy-start(f32[12,512,128]{2,1,0:T(8,128)} %copy-done) | copy-start | bytes 9437188
  295.4 9.0 %copy-start.25 = (f32[1,512]{1,0:T(1,128)S(1)}, f32[1,512]{1,0:T(1,128)}, u32[]{:S(2)}) copy-start(f32[1,512]{1,0:T(1,128)} %copy-done.24) | copy-start | bytes 6148
  295.4 2.2 collective-permute-start.31
  (38 other events, 219.8 us)
Sparse Core Ops, SparseCore 0:
  9.5 14.0 all-gather.1
